TPU v7x, 512 devices: a whole 4x4x16 slice. The times are simulated.
512 devices in a mesh: dp: 32 (over z, core), freq: 16 (over x, y).
Axes of the slice: x: 4, y: 4, z: 16, core: 2. Of those that a mesh axis runs over, the one named last changes fastest.
Arguments:
- output_grad: bfloat16 [1024, 384, 1024], P(('dp', 'freq')), may hold values from -6 to 6
- layer_input: bfloat16 [1024, 384, 1024], P(('dp', 'freq')), may hold values from -6 to 6
- counts: int32 [512], P(('dp', 'freq')), may hold values from 0 to 2, as said below
- bin_order: int32 [64], replicated, may hold values from 0 to 1023, as said below
- inverse_factor: bfloat16 [64, 2, 384, 384], P('freq'), may hold values from -0.10306207 to 0.70406207
Outputs:
- input_spectra_grad: bfloat16 [1024, 128, 384], P(('dp', 'freq'))
- tap_grad: float32 [9, 384, 384], P(None, 'dp', 'freq')
Inputs may be any that keep to these rules, and one draw needn't show every extreme that they name: `counts`: slots at or past a shard's count hold no image; some shard has all 2 slots live and some has none. `bin_order`: entries are distinct bins of the 32 x 32 grid; slot j belongs to freq index j // 4.
All inputs are finite; a program needn't handle non-finite values.
Results may differ from a plain program's by a relative error of at most 0.0071.
Values may be sent and summed in bfloat16 or wider, within the bound.
No kernel may reach another device: no remote copies, remote signals or barrier semaphores. Data moves between devices by JAX's collectives and lax.ppermute only.
A program may use at most 64 MiB of HBM per device.

v0:
```python
import math
import jax
import jax.numpy as jnp
from jax import lax
from jax.sharding import Mesh, PartitionSpec as P

GRID = 32


def dft_table(bin_order, grid_side):
    pixel_index = jnp.arange(grid_side * grid_side, dtype=jnp.int32)
    row_pos = pixel_index // grid_side
    col_pos = pixel_index % grid_side
    freq_u = bin_order // grid_side
    freq_v = bin_order % grid_side
    phase_turns = (
        row_pos[:, None] * freq_u[None, :] + col_pos[:, None] * freq_v[None, :]
    ) % grid_side
    phase_angle = phase_turns.astype(jnp.float32) * (2.0 * math.pi / grid_side)
    both_parts = jnp.stack([jnp.cos(phase_angle), -jnp.sin(phase_angle)], axis=2) / grid_side
    return both_parts.reshape(grid_side * grid_side, -1).astype(jnp.bfloat16)


def tap_phases(bin_order, grid_side):
    offsets = jnp.arange(9, dtype=jnp.int32)
    shift_y = offsets // 3 - 1
    shift_x = offsets % 3 - 1
    freq_u = bin_order // grid_side
    freq_v = bin_order % grid_side
    phase_turns = (
        freq_u[:, None] * shift_y[None, :] + freq_v[:, None] * shift_x[None, :]
    ) % grid_side
    phase_angle = phase_turns.astype(jnp.float32) * (2.0 * math.pi / grid_side)
    return (jnp.cos(phase_angle), jnp.sin(phase_angle))


def local(output_grad, layer_input, counts, bin_order, inverse_factor):
    slot_count, channels, pixels = output_grad.shape
    freq_devices = lax.axis_size("freq")
    data_devices = lax.axis_size("z") * lax.axis_size("c")
    bins_local = inverse_factor.shape[0]
    total_bins = bin_order.shape[0]
    live_mask = (jnp.arange(slot_count, dtype=jnp.int32) < counts[0]).astype(jnp.bfloat16)
    bins_table = dft_table(bin_order, GRID)

    def spectrum(images):
        masked = images * live_mask[:, None, None]
        return jnp.einsum(
            "scp,pk->skc", masked, bins_table, preferred_element_type=jnp.float32
        ).astype(jnp.bfloat16)

    both_spec = jnp.stack([spectrum(output_grad), spectrum(layer_input)], axis=0)
    both_recv = lax.all_to_all(both_spec, "freq", split_axis=2, concat_axis=1, tiled=True)
    image_rows = both_recv.shape[1]
    parts = both_recv.reshape(2, image_rows, bins_local, 2, channels)
    grad_real = parts[0, :, :, 0]
    grad_imag = parts[0, :, :, 1]
    input_real = parts[1, :, :, 0]
    input_imag = parts[1, :, :, 1]
    factor_real = inverse_factor[:, 0]
    factor_imag = inverse_factor[:, 1]
    f32 = jnp.float32

    def mm(x, p, eq):
        return jnp.einsum(eq, x, p, preferred_element_type=f32)

    u_real = mm(grad_real, factor_real, "ibr,brc->ibc") + mm(grad_imag, factor_imag, "ibr,brc->ibc")
    u_imag = mm(grad_imag, factor_real, "ibr,brc->ibc") - mm(grad_real, factor_imag, "ibr,brc->ibc")
    back_real = 2.0 * u_real - grad_real.astype(f32)
    back_imag = 2.0 * u_imag - grad_imag.astype(f32)
    back_both = (
        jnp.stack([back_real, back_imag], axis=2)
        .astype(jnp.bfloat16)
        .reshape(image_rows, 2 * bins_local, channels)
    )
    returned = lax.all_to_all(back_both, "freq", split_axis=0, concat_axis=1, tiled=True)
    v_real = mm(input_real, factor_real, "ibk,bck->ibc") - mm(
        input_imag, factor_imag, "ibk,bck->ibc"
    )
    v_imag = mm(input_real, factor_imag, "ibk,bck->ibc") + mm(
        input_imag, factor_real, "ibk,bck->ibc"
    )
    local_bins = lax.dynamic_slice_in_dim(
        bin_order, lax.axis_index("freq") * bins_local, bins_local
    )
    cos_local, sin_local = tap_phases(local_bins, GRID)
    cos_t = cos_local.T[:, None, :, None]
    sin_t = sin_local.T[:, None, :, None]
    ur = u_real[None]
    ui = u_imag[None]
    z_t = jnp.stack([cos_t * ur - sin_t * ui, cos_t * ui + sin_t * ur], axis=1).astype(jnp.bfloat16)
    w_t = jnp.stack([cos_t * ur + sin_t * ui, cos_t * ui - sin_t * ur], axis=1).astype(jnp.bfloat16)
    y_all = jnp.stack([v_real, v_imag], axis=0).astype(jnp.bfloat16)
    taps = z_t.shape[0]
    col_share = channels // freq_devices
    row_share = channels // data_devices
    y_cols = y_all.reshape(2, image_rows, bins_local, freq_devices, col_share)
    w_cols = w_t.reshape(taps, 2, image_rows, bins_local, freq_devices, col_share)
    first = jnp.einsum("teibr,eibfc->ftrc", z_t, y_cols, preferred_element_type=f32)
    second = jnp.einsum("eibr,teibfc->ftrc", y_all, w_cols, preferred_element_type=f32)
    gram_scale = 1.0 / math.sqrt(data_devices * freq_devices * slot_count)
    tap_scale = 2.0 * gram_scale / math.sqrt(total_bins)
    col_pieces = ((second - first) * tap_scale).astype(jnp.bfloat16)
    col_pieces = lax.all_to_all(col_pieces, "freq", split_axis=0, concat_axis=0, tiled=True)
    col_sum = jnp.sum(col_pieces.astype(f32), axis=0)
    z_devices = lax.axis_size("z")
    core_devices = lax.axis_size("c")
    row_pieces = jnp.transpose(
        col_sum.astype(jnp.bfloat16).reshape(taps, z_devices, core_devices, row_share, col_share),
        (2, 1, 0, 3, 4),
    )
    row_pieces = lax.all_to_all(row_pieces, "c", split_axis=0, concat_axis=0, tiled=True)
    row_pieces = jnp.sum(row_pieces.astype(f32), axis=0).astype(jnp.bfloat16)
    row_pieces = lax.all_to_all(row_pieces, "z", split_axis=0, concat_axis=0, tiled=True)
    tap_grad = jnp.sum(row_pieces.astype(f32), axis=0)
    return (returned, tap_grad)


def solution(mesh):
    cores = 2
    chips = Mesh(
        mesh.devices.reshape(mesh.shape["dp"] // cores, cores, mesh.shape["freq"]),
        ("z", "c", "freq"),
    )
    return jax.shard_map(
        local,
        mesh=chips,
        in_specs=(
            P(("z", "c", "freq"), None, None),
            P(("z", "c", "freq"), None, None),
            P(("z", "c", "freq")),
            P(),
            P("freq", None, None, None),
        ),
        out_specs=(P(("z", "c", "freq"), None, None), P(None, ("z", "c"), "freq")),
        check_vma=False,
    )
```

profile of v0, /device:TPU:8, one launch (start us, length us, event | category | flops | bytes accessed | tf_op | source)
XLA Modules:
  0.0 136.7 jit_solution(17668139572337699015)
XLA Ops:
  1.4 0.7 and_select_fusion.5
  2.1 1.1 fusion.84
  3.3 0.3 copy.109
  3.7 0.7 fusion.37
  4.4 2.1 %fusion.40 = bf16[1,2,128,384]{3,2,1,0:T(8,128)(2,1)S(1)} fusion(bf16[1024,128,1]{0,1,2:T(8,128)(2,1)S(1)} %reshape.456, bf16[2,384,1024]{2,1,0:T(8,128)(2,1)} %param.5, bf16[2]{0:T(256)(128)(2,1)S(1)} %compare_convert_fusion), kind=kOutput, calls=%fused_computation.38 | convolution fusion | flops 204570624 | bytes 2031620 | tf_op jit(solution)/shard_map/scp,pk->skc/dot_general | solution.py:48
  6.6 1.2 copy.110
  7.8 9.2 %all-to-all-start = ((bf16[2,2,128,384]{3,1,0,2:T(2,128)(2,1)}), bf16[2,2,128,384]{3,1,0,2:T(2,128)(2,1)S(1)}, u32[]{:S(2)}, u32[]{:S(2)}) async-start(bf16[2,2,128,384]{3,1,0,2:T(2,128)(2,1)} %copy.110), calls=%async_computation | async-start | bytes 786432 | tf_op jit(solution)/shard_map/all_to_all | solution.py:53
  17.2 7.4 %all-to-all-done = bf16[2,2,128,384]{3,1,0,2:T(2,128)(2,1)S(1)} async-done(((bf16[2,2,128,384]{3,1,0,2:T(2,128)(2,1)}), bf16[2,2,128,384]{3,1,0,2:T(2,128)(2,1)S(1)}, u32[]{:S(2)}, u32[]{:S(2)}) %all-to-all-start) | async-done | bytes 393248 | tf_op jit(solution)/shard_map/all_to_all | solution.py:53
  24.5 0.3 copy.111
  24.8 0.6 fusion.103
  25.4 0.4 fusion.17
  25.9 0.5 fusion.15
  26.3 0.5 fusion.64
  26.8 0.5 fusion.61
  27.4 0.3 fusion.21
  27.6 0.3 fusion.19
  27.9 0.3 fusion.46
  28.2 0.3 fusion.52
  28.5 0.7 stack.66
  29.2 1.3 copy.124
  30.5 0.7 stack.67
  31.2 1.3 copy.125
  32.4 0.6 mul.328
  33.1 0.5 copy.120
  33.6 0.6 mul.324
  34.2 0.5 copy.119
  34.7 0.7 subtract_convert_fusion.1
  35.4 2.0 %add_convert_fusion = (bf16[9,1,32,4,16,24]{2,5,1,3,4,0:T(8,128)(2,1)S(1)}, bf16[9,1,32,4,16,24]{2,5,1,3,4,0:T(8,128)(2,1)S(1)}) fusion(f32[32,4,16,24]{0,3,1,2:T(8,128)S(1)} %copy.120, f32[9,4]{1,0:T(8,128)S(1)} %get-tuple-element.21, f32[32,4,16,24]{0,3,1,2:T(8,128)S(1)} %copy.119, f32[9,4]{1,0:T(8,128)S(1)} %get-tuple-element.20), kind=kLoop, calls=%fused_computation.5 | loop fusion | flops 3538944 | bytes 2162976 | tf_op jit(solution)/shard_map/convert.12
  37.5 1.1 fusion.8
  38.6 4.4 %fusion.5 = bf16[16,9,384,24]{2,3,0,1:T(8,128)(2,1)S(1)} fusion(f32[16,24,9,384,1,1]{3,1,5,4,0,2:T(8,128)S(1)} %fusion.8, bf16[9,1,32,4,16,24]{2,5,1,3,4,0:T(8,128)(2,1)S(1)} %get-tuple-element.11, bf16[9,1,32,4,16,24]{2,5,1,3,4,0:T(8,128)(2,1)S(1)} %get-tuple-element.10, bf16[1,32,4,384]{3,1,2,0:T(8,128)(2,1)S(1)} %bitcast.148, ...), kind=kOutput, calls=%fused_computation.8 | convolution fusion | flops 684441600 | bytes 9928704 | tf_op jit(solution)/shard_map/eibr,teibfc->ftrc/dot_general | solution.py:100
  43.0 1.8 %copy.126 = bf16[16,9,384,24]{2,3,1,0:T(8,128)(2,1)} copy(bf16[16,9,384,24]{2,3,0,1:T(8,128)(2,1)S(1)} %fusion.5) | data formatting | bytes 5308416 | tf_op jit(solution)/shard_map/convert_element_type | solution.py:103
  44.8 5.3 %all-to-all-start.2 = ((bf16[16,9,384,24]{2,3,1,0:T(8,128)(2,1)}), bf16[16,9,384,24]{2,3,1,0:T(8,128)(2,1)S(1)}, u32[]{:S(2)}, u32[]{:S(2)}) async-start(bf16[16,9,384,24]{2,3,1,0:T(8,128)(2,1)} %copy.126), calls=%async_computation.2 | async-start | bytes 5308416 | tf_op jit(solution)/shard_map/all_to_all | solution.py:104
  50.3 0.7 copy.117
  51.0 31.2 %all-to-all-done.2 = bf16[16,9,384,24]{2,3,1,0:T(8,128)(2,1)S(1)} async-done(((bf16[16,9,384,24]{2,3,1,0:T(8,128)(2,1)}), bf16[16,9,384,24]{2,3,1,0:T(8,128)(2,1)S(1)}, u32[]{:S(2)}, u32[]{:S(2)}) %all-to-all-start.2) | async-done | bytes 2654240 | tf_op jit(solution)/shard_map/all_to_all | solution.py:104
  82.2 0.4 reduce_sum.33
  82.6 4.0 %reshape.455 = bf16[9,16,2,12,24]{3,2,1,4,0:T(2,128)(2,1)S(1)} reshape(bf16[9,384,24]{1,2,0:T(8,128)(2,1)S(1)} %reduce_sum.33) | data formatting | bytes 331776 | tf_op jit(solution)/shard_map/reshape | solution.py:109
  86.6 2.6 %copy.127 = bf16[2,16,9,12,24]{4,1,3,2,0:T(8,128)(2,1)S(1)} copy(bf16[2,16,9,12,24]{3,0,1,4,2:T(2,128)(2,1)S(1)} %bitcast.139) | data formatting | bytes 331776 | tf_op jit(solution)/shard_map/transpose | solution.py:108
  89.3 1.2 reshape.463
  90.4 3.8 %all_to_all.48 = bf16[2,2,20736]{2,1,0:T(2,128)(2,1)S(1)} all-to-all(bf16[2,2,20736]{2,1,0:T(2,128)(2,1)S(1)} %reshape.463), channel_id=1, replica_groups=mesh['z'=16,'c'=2,'freq'=16] {'c'}, dimensions={0} | all-to-all | bytes 331776 | tf_op jit(solution)/shard_map/all_to_all | solution.py:112
  94.3 6.0 %all-to-all-start.1 = ((bf16[32,8,384]{2,1,0:T(8,128)(2,1)}), bf16[32,8,384]{2,1,0:T(8,128)(2,1)S(1)}, u32[]{:S(2)}, u32[]{:S(2)}) async-start(bf16[32,8,384]{2,1,0:T(8,128)(2,1)} %copy.117), calls=%async_computation.1 | async-start | bytes 393216 | tf_op jit(solution)/shard_map/all_to_all | solution.py:76
  100.3 1.2 reshape.464
  101.9 1.2 reshape.465
  103.1 4.0 %all-to-all-done.1 = bf16[32,8,384]{2,1,0:T(8,128)(2,1)S(1)} async-done(((bf16[32,8,384]{2,1,0:T(8,128)(2,1)}), bf16[32,8,384]{2,1,0:T(8,128)(2,1)S(1)}, u32[]{:S(2)}, u32[]{:S(2)}) %all-to-all-start.1) | async-done | bytes 196640 | tf_op jit(solution)/shard_map/all_to_all | solution.py:76
  107.1 15.2 %all-to-all-start.4 = ((bf16[16,2,1296]{2,1,0:T(2,128)(2,1)}), bf16[16,2,1296]{2,1,0:T(2,128)(2,1)S(1)}, u32[]{:S(2)}, u32[]{:S(2)}) async-start(bf16[16,2,1296]{2,1,0:T(2,128)(2,1)} %reshape.465), calls=%async_computation.4 | async-start | bytes 180224 | tf_op jit(solution)/shard_map/all_to_all | solution.py:114
  122.3 0.7 copy.168
  123.0 12.2 %all-to-all-done.4 = bf16[16,2,1296]{2,1,0:T(2,128)(2,1)S(1)} async-done(((bf16[16,2,1296]{2,1,0:T(2,128)(2,1)}), bf16[16,2,1296]{2,1,0:T(2,128)(2,1)S(1)}, u32[]{:S(2)}, u32[]{:S(2)}) %all-to-all-start.4) | async-done | bytes 82976 | tf_op jit(solution)/shard_map/all_to_all | solution.py:114
  135.3 0.6 reshape.466
  135.9 0.9 convert_reduce_fusion
  (29 shorter events, 0.9 us)
Async XLA Ops:
  0.6 3.0 %copy-start.6 = (bf16[2,384,1024]{2,1,0:T(8,128)(2,1)S(1)}, bf16[2,384,1024]{2,1,0:T(8,128)(2,1)}, u32[]{:S(2)}) copy-start(bf16[2,384,1024]{2,1,0:T(8,128)(2,1)} %param.6) | copy-start | bytes 4718596
  4.4 12.5 %copy-start.5 = (s32[64]{0:T(128)S(1)}, s32[64]{0:T(128)}, u32[]{:S(2)}) copy-start(s32[64]{0:T(128)} %param.8) | copy-start | bytes 772
  6.6 18.9 %copy-start = (bf16[4,2,384,384]{3,2,1,0:T(8,128)(2,1)S(1)}, bf16[4,2,384,384]{3,2,1,0:T(8,128)(2,1)}, u32[]{:S(2)}) copy-start(bf16[4,2,384,384]{3,2,1,0:T(8,128)(2,1)} %param.9) | copy-start | bytes 7077892
  7.8 16.8 %all-to-all-start = ((bf16[2,2,128,384]{3,1,0,2:T(2,128)(2,1)}), bf16[2,2,128,384]{3,1,0,2:T(2,128)(2,1)S(1)}, u32[]{:S(2)}, u32[]{:S(2)}) async-start(bf16[2,2,128,384]{3,1,0,2:T(2,128)(2,1)} %copy.110), calls=%async_computation | async-start | bytes 786432 | tf_op jit(solution)/shard_map/all_to_all | solution.py:53
  27.3 3.2 %copy-start.3 = (bf16[4,32,384]{2,1,0:T(8,128)(2,1)}, bf16[4,32,384]{2,1,0:T(8,128)(2,1)S(1)}, u32[]{:S(2)}) copy-start(bf16[4,32,384]{2,1,0:T(8,128)(2,1)S(1)} %fusion.61) | copy-start | bytes 294916
  35.4 2.0 %copy-start.1 = (bf16[1,32,4,16,24]{1,4,0,2,3:T(8,128)(2,1)S(1)}, bf16[1,32,4,16,24]{1,4,0,2,3:T(8,128)(2,1)}, u32[]{:S(2)}) copy-start(bf16[1,32,4,16,24]{1,4,0,2,3:T(8,128)(2,1)} %copy.124) | copy-start | bytes 294916
  35.4 2.0 %copy-start.2 = (bf16[1,32,4,16,24]{1,4,0,2,3:T(8,128)(2,1)S(1)}, bf16[1,32,4,16,24]{1,4,0,2,3:T(8,128)(2,1)}, u32[]{:S(2)}) copy-start(bf16[1,32,4,16,24]{1,4,0,2,3:T(8,128)(2,1)} %copy.125) | copy-start | bytes 294916
  37.5 1.1 copy-start.4
  44.8 37.4 %all-to-all-start.2 = ((bf16[16,9,384,24]{2,3,1,0:T(8,128)(2,1)}), bf16[16,9,384,24]{2,3,1,0:T(8,128)(2,1)S(1)}, u32[]{:S(2)}, u32[]{:S(2)}) async-start(bf16[16,9,384,24]{2,3,1,0:T(8,128)(2,1)} %copy.126), calls=%async_computation.2 | async-start | bytes 5308416 | tf_op jit(solution)/shard_map/all_to_all | solution.py:104
  94.3 12.8 %all-to-all-start.1 = ((bf16[32,8,384]{2,1,0:T(8,128)(2,1)}), bf16[32,8,384]{2,1,0:T(8,128)(2,1)S(1)}, u32[]{:S(2)}, u32[]{:S(2)}) async-start(bf16[32,8,384]{2,1,0:T(8,128)(2,1)} %copy.117), calls=%async_computation.1 | async-start | bytes 393216 | tf_op jit(solution)/shard_map/all_to_all | solution.py:76
  107.1 28.1 %all-to-all-start.4 = ((bf16[16,2,1296]{2,1,0:T(2,128)(2,1)}), bf16[16,2,1296]{2,1,0:T(2,128)(2,1)S(1)}, u32[]{:S(2)}, u32[]{:S(2)}) async-start(bf16[16,2,1296]{2,1,0:T(2,128)(2,1)} %reshape.465), calls=%async_computation.4 | async-start | bytes 180224 | tf_op jit(solution)/shard_map/all_to_all | solution.py:114
where the time goes:
time: 137 us
  waiting for transfers between devices  54.9 us (40%)
  starting transfers between devices  35.7 us (26%)
  local copies, waits for them, and re-layouts  22.8 us (17%)
  matrix products  11.4 us (8%)
  other arithmetic  6.38 us (5%)
  blocking collectives  3.85 us (3%)
  between operations  1.78 us (1%)
    all_to_all x1, waiting for transfers between devices, local(): lax.all_to_all(col_pieces, 'freq', split_axis=0, concat_axis=0, tiled=True)  31.2 us
    all_to_all x1, starting transfers between devices, local(): lax.all_to_all(row_pieces, 'z', split_axis=0, concat_axis=0, tiled=True)  15.2 us
    all_to_all x1, waiting for transfers between devices, local(): lax.all_to_all(row_pieces, 'z', split_axis=0, concat_axis=0, tiled=True)  12.2 us
    all_to_all x1, starting transfers between devices, local(): lax.all_to_all(both_spec, 'freq', split_axis=2, concat_axis=1, tiled=True)  9.16 us
    all_to_all x1, waiting for transfers between devices, local(): lax.all_to_all(both_spec, 'freq', split_axis=2, concat_axis=1, tiled=True)  7.36 us
    all_to_all x1, starting transfers between devices, local(): lax.all_to_all(back_both, 'freq', split_axis=0, concat_axis=1, tiled=True)  6.01 us
    all_to_all x1, starting transfers between devices, local(): lax.all_to_all(col_pieces, 'freq', split_axis=0, concat_axis=0, tiled=True)  5.34 us
    dot_general x1, matrix products, local(): jnp.einsum('eibr,teibfc->ftrc', y_all, w_cols, preferred_element_type=f32)  4.44 us
  transfers between devices with their start and end apart: 4, of which 4 were waited for; matrix products, arithmetic and copies ran while one was open for 3% of the time, Pallas kernels for 0%

commit v1 on v0

--- a/solution.py
+++ b/solution.py
@@ -73,7 +73,18 @@
         .astype(jnp.bfloat16)
         .reshape(image_rows, 2 * bins_local, channels)
     )
-    returned = lax.all_to_all(back_both, "freq", split_axis=0, concat_axis=1, tiled=True)
+    ways, here = (lax.axis_size("freq"), lax.axis_index("freq"))
+    width = back_both.shape[0] // ways
+    shape = list(back_both.shape)
+    shape[0] = width
+    height = shape[1]
+    shape[1] = height * ways
+    returned = jnp.zeros(shape, back_both.dtype)
+    for mask in range(ways):
+        part = lax.dynamic_slice_in_dim(back_both, (here ^ mask) * width, width, axis=0)
+        if mask:
+            part = lax.ppermute(part, "freq", [(d, d ^ mask) for d in range(ways)])
+        returned = lax.dynamic_update_slice_in_dim(returned, part, (here ^ mask) * height, axis=1)
     v_real = mm(input_real, factor_real, "ibk,bck->ibc") - mm(
         input_imag, factor_imag, "ibk,bck->ibc"
     )

time: 137 us -> 229 us (1.67)
  the two profiles are of different devices: /device:TPU:8 before, /device:TPU:26 now
where the time goes in v1:
time: 229 us; the launch traced here: 228 us
  starting transfers between devices  84.3 us (37%)
  waiting for transfers between devices  80.4 us (35%)
  local copies, waits for them, and re-layouts  29.7 us (13%)
  matrix products  17 us (7%)
  other arithmetic  10.6 us (5%)
  blocking collectives  3.85 us (2%)
  between operations  2.29 us (1%)
    ppermute x15, waiting for transfers between devices, local(): part = lax.ppermute(part, 'freq', [(d, d ^ mask) for d in range(ways)])  62.9 us
    ppermute x15, starting transfers between devices, local(): part = lax.ppermute(part, 'freq', [(d, d ^ mask) for d in range(ways)])  48.9 us
    all_to_all x1, starting transfers between devices, local(): lax.all_to_all(row_pieces, 'z', split_axis=0, concat_axis=0, tiled=True)  17.4 us
    all_to_all x1, waiting for transfers between devices, local(): lax.all_to_all(row_pieces, 'z', split_axis=0, concat_axis=0, tiled=True)  12.2 us
    all_to_all x1, starting transfers between devices, local(): lax.all_to_all(col_pieces, 'freq', split_axis=0, concat_axis=0, tiled=True)  9.04 us
    all_to_all x1, starting transfers between devices, local(): lax.all_to_all(both_spec, 'freq', split_axis=2, concat_axis=1, tiled=True)  8.95 us
    dot_general x8, matrix products, mm(): return jnp.einsum(eq, x, p, preferred_element_type=f32)  8.62 us
    all_to_all x1, waiting for transfers between devices, local(): lax.all_to_all(both_spec, 'freq', split_axis=2, concat_axis=1, tiled=True)  5.23 us
  transfers between devices with their start and end apart: 18, of which 12 were waited for; matrix products, arithmetic and copies ran while one was open for 14% of the time, Pallas kernels for 0%

profile of v1, /device:TPU:26, one launch (start us, length us, event | category | flops | bytes accessed | tf_op | source)
XLA Modules:
  0.0 228.2 jit_solution(9705594292170274228)
XLA Ops:
  4.4 2.1 fusion.40
  7.8 8.9 %all-to-all-start = ((bf16[2,2,128,384]{3,1,0,2:T(2,128)(2,1)}), bf16[2,2,128,384]{3,1,0,2:T(2,128)(2,1)S(1)}, u32[]{:S(2)}, u32[]{:S(2)}) async-start(bf16[2,2,128,384]{3,1,0,2:T(2,128)(2,1)} %copy.152), calls=%async_computation | async-start | bytes 786432 | tf_op jit(solution)/shard_map/all_to_all | solution.py:53
  17.2 5.2 %all-to-all-done = bf16[2,2,128,384]{3,1,0,2:T(2,128)(2,1)S(1)} async-done(((bf16[2,2,128,384]{3,1,0,2:T(2,128)(2,1)}), bf16[2,2,128,384]{3,1,0,2:T(2,128)(2,1)S(1)}, u32[]{:S(2)}, u32[]{:S(2)}) %all-to-all-start) | async-done | bytes 393248 | tf_op jit(solution)/shard_map/all_to_all | solution.py:53
  22.8 1.3 fusion.103
  26.3 1.6 fusion.86
  27.9 1.6 mul.456
  29.4 2.0 fusion.46
  31.4 1.7 fusion.85
  33.1 2.6 %mul.452 = f32[32,4,16,24]{3,2,0,1:T(8,128)} reshape(f32[32,4,384]{2,0,1:T(8,128)} %fusion.46) | data formatting | bytes 393216 | tf_op jit(solution)/shard_map/mul | solution.py:103
  35.7 1.4 fusion.17
  37.2 1.4 fusion.15
  41.2 4.7 %collective-permute-start.14 = (bf16[2,8,384]{2,0,1:T(2,128)(2,1)S(1)}, bf16[2,8,384]{2,0,1:T(2,128)(2,1)}, u32[]{:S(2)}, u32[]{:S(2)}) collective-permute-start(bf16[2,8,384]{2,0,1:T(2,128)(2,1)S(1)} %get-tuple-element.18), channel_id=1, source_target_pairs={{0,15},{1,14},{2,13},{3,12},{4,11},{5,10},{6,9},{7,8},{8,7},{9,6},... | collective-permute-start | bytes 36872 | tf_op jit(solution)/shard_map/ppermute | solution.py:86
  45.9 3.2 %collective-permute-start.13 = (bf16[2,8,384]{2,0,1:T(2,128)(2,1)}, bf16[2,8,384]{2,0,1:T(2,128)(2,1)}, u32[]{:S(2)}, u32[]{:S(2)}) collective-permute-start(bf16[2,8,384]{2,0,1:T(2,128)(2,1)} %get-tuple-element.19), channel_id=1, source_target_pairs={{0,14},{1,15},{2,12},{3,13},{4,10},{5,11},{6,8},{7,9},{8,6},{9,7},... | collective-permute-start | bytes 36872 | tf_op jit(solution)/shard_map/ppermute | solution.py:86
  49.2 3.3 %collective-permute-start.12 = (bf16[2,8,384]{2,0,1:T(2,128)(2,1)}, bf16[2,8,384]{2,0,1:T(2,128)(2,1)}, u32[]{:S(2)}, u32[]{:S(2)}) collective-permute-start(bf16[2,8,384]{2,0,1:T(2,128)(2,1)} %get-tuple-element.20), channel_id=1, source_target_pairs={{0,13},{1,12},{2,15},{3,14},{4,9},{5,8},{6,11},{7,10},{8,5},{9,4},... | collective-permute-start | bytes 36872 | tf_op jit(solution)/shard_map/ppermute | solution.py:86
  52.5 2.8 %collective-permute-start.11 = (bf16[2,8,384]{2,0,1:T(2,128)(2,1)}, bf16[2,8,384]{2,0,1:T(2,128)(2,1)}, u32[]{:S(2)}, u32[]{:S(2)}) collective-permute-start(bf16[2,8,384]{2,0,1:T(2,128)(2,1)} %get-tuple-element.21), channel_id=1, source_target_pairs={{0,12},{1,13},{2,14},{3,15},{4,8},{5,9},{6,10},{7,11},{8,4},{9,5},... | collective-permute-start | bytes 36872 | tf_op jit(solution)/shard_map/ppermute | solution.py:86
  55.4 3.3 %collective-permute-start = (bf16[2,8,384]{2,0,1:T(2,128)(2,1)}, bf16[2,8,384]{2,0,1:T(2,128)(2,1)}, u32[]{:S(2)}, u32[]{:S(2)}) collective-permute-start(bf16[2,8,384]{2,0,1:T(2,128)(2,1)} %get-tuple-element.32), channel_id=1, source_target_pairs={{0,1},{1,0},{2,3},{3,2},{4,5},{5,4},{6,7},{7,6},{8,9},{9,8},{10,11... | collective-permute-start | bytes 36872 | tf_op jit(solution)/shard_map/ppermute | solution.py:86
  59.3 1.3 copy.180
  61.3 1.3 copy.181
  63.5 1.7 subtract_convert_fusion.1
  65.3 2.0 add_convert_fusion
  68.4 4.4 %fusion.5 = bf16[16,9,384,24]{2,3,0,1:T(8,128)(2,1)S(1)} fusion(f32[16,24,9,384,1,1]{3,1,5,4,0,2:T(8,128)S(1)} %fusion.8, bf16[9,1,32,4,16,24]{2,5,1,3,4,0:T(8,128)(2,1)S(1)} %get-tuple-element.11, bf16[9,1,32,4,16,24]{2,5,1,3,4,0:T(8,128)(2,1)S(1)} %get-tuple-element.10, bf16[1,32,4,384]{3,1,2,0:T(8,128)(2,1)S(1)} %bitcast.141, ...), kind=kOutput, calls=%fused_computation.8 | convolution fusion | flops 684441600 | bytes 9928704 | tf_op jit(solution)/shard_map/eibr,teibfc->ftrc/dot_general | solution.py:111
  72.8 1.8 copy.182
  74.7 9.0 %all-to-all-start.1 = ((bf16[16,9,384,24]{2,3,1,0:T(8,128)(2,1)}), bf16[16,9,384,24]{2,3,1,0:T(8,128)(2,1)S(1)}, u32[]{:S(2)}, u32[]{:S(2)}) async-start(bf16[16,9,384,24]{2,3,1,0:T(8,128)(2,1)} %copy.182), calls=%async_computation.1 | async-start | bytes 5308416 | tf_op jit(solution)/shard_map/all_to_all | solution.py:115
  83.8 3.4 %collective-permute-start.1 = (bf16[2,8,384]{2,0,1:T(2,128)(2,1)S(1)}, bf16[2,8,384]{2,0,1:T(2,128)(2,1)S(1)}, u32[]{:S(2)}, u32[]{:S(2)}) collective-permute-start(bf16[2,8,384]{2,0,1:T(2,128)(2,1)S(1)} %copy-done.21), channel_id=1, source_target_pairs={{0,2},{1,3},{2,0},{3,1},{4,6},{5,7},{6,4},{7,5},{8,10},{9,11},{10,... | collective-permute-start | bytes 36872 | tf_op jit(solution)/shard_map/ppermute | solution.py:86
  87.9 21.6 %collective-permute-done.1 = bf16[2,8,384]{2,0,1:T(2,128)(2,1)S(1)} collective-permute-done((bf16[2,8,384]{2,0,1:T(2,128)(2,1)S(1)}, bf16[2,8,384]{2,0,1:T(2,128)(2,1)S(1)}, u32[]{:S(2)}, u32[]{:S(2)}) %collective-permute-start.1) | collective-permute-done | bytes 12320 | tf_op jit(solution)/shard_map/ppermute | solution.py:86
  109.5 1.9 collective-permute-start.2
  111.5 4.9 %collective-permute-done.2 = bf16[2,8,384]{2,0,1:T(2,128)(2,1)S(1)} collective-permute-done((bf16[2,8,384]{2,0,1:T(2,128)(2,1)S(1)}, bf16[2,8,384]{2,0,1:T(2,128)(2,1)S(1)}, u32[]{:S(2)}, u32[]{:S(2)}) %collective-permute-start.2) | collective-permute-done | bytes 12320 | tf_op jit(solution)/shard_map/ppermute | solution.py:86
  116.3 1.9 collective-permute-start.3
  118.3 3.6 %collective-permute-done.3 = bf16[2,8,384]{2,0,1:T(2,128)(2,1)S(1)} collective-permute-done((bf16[2,8,384]{2,0,1:T(2,128)(2,1)S(1)}, bf16[2,8,384]{2,0,1:T(2,128)(2,1)S(1)}, u32[]{:S(2)}, u32[]{:S(2)}) %collective-permute-start.3) | collective-permute-done | bytes 12320 | tf_op jit(solution)/shard_map/ppermute | solution.py:86
  121.9 1.9 collective-permute-start.4
  123.8 4.5 %collective-permute-done.4 = bf16[2,8,384]{2,0,1:T(2,128)(2,1)S(1)} collective-permute-done((bf16[2,8,384]{2,0,1:T(2,128)(2,1)S(1)}, bf16[2,8,384]{2,0,1:T(2,128)(2,1)S(1)}, u32[]{:S(2)}, u32[]{:S(2)}) %collective-permute-start.4) | collective-permute-done | bytes 12320 | tf_op jit(solution)/shard_map/ppermute | solution.py:86
  128.4 1.9 collective-permute-start.5
  130.3 6.0 %collective-permute-done.5 = bf16[2,8,384]{2,0,1:T(2,128)(2,1)S(1)} collective-permute-done((bf16[2,8,384]{2,0,1:T(2,128)(2,1)S(1)}, bf16[2,8,384]{2,0,1:T(2,128)(2,1)S(1)}, u32[]{:S(2)}, u32[]{:S(2)}) %collective-permute-start.5) | collective-permute-done | bytes 12320 | tf_op jit(solution)/shard_map/ppermute | solution.py:86
  136.4 1.9 collective-permute-start.6
  138.3 5.8 %collective-permute-done.6 = bf16[2,8,384]{2,0,1:T(2,128)(2,1)S(1)} collective-permute-done((bf16[2,8,384]{2,0,1:T(2,128)(2,1)S(1)}, bf16[2,8,384]{2,0,1:T(2,128)(2,1)S(1)}, u32[]{:S(2)}, u32[]{:S(2)}) %collective-permute-start.6) | collective-permute-done | bytes 12320 | tf_op jit(solution)/shard_map/ppermute | solution.py:86
  144.1 6.9 %collective-permute-start.7 = (bf16[2,8,384]{2,0,1:T(2,128)(2,1)S(1)}, bf16[2,8,384]{2,0,1:T(2,128)(2,1)S(1)}, u32[]{:S(2)}, u32[]{:S(2)}) collective-permute-start(bf16[2,8,384]{2,0,1:T(2,128)(2,1)S(1)} %copy-done.15), channel_id=1, source_target_pairs={{0,8},{1,9},{2,10},{3,11},{4,12},{5,13},{6,14},{7,15},{8,0},{9,1},... | collective-permute-start | bytes 36872 | tf_op jit(solution)/shard_map/ppermute | solution.py:86
  151.0 1.6 collective-permute-done.7
  152.6 3.3 %collective-permute-start.8 = (bf16[2,8,384]{2,0,1:T(2,128)(2,1)S(1)}, bf16[2,8,384]{2,0,1:T(2,128)(2,1)S(1)}, u32[]{:S(2)}, u32[]{:S(2)}) collective-permute-start(bf16[2,8,384]{2,0,1:T(2,128)(2,1)S(1)} %copy-done.14), channel_id=1, source_target_pairs={{0,9},{1,8},{2,11},{3,10},{4,13},{5,12},{6,15},{7,14},{8,1},{9,0},... | collective-permute-start | bytes 36872 | tf_op jit(solution)/shard_map/ppermute | solution.py:86
  156.0 4.6 %collective-permute-done.8 = bf16[2,8,384]{2,0,1:T(2,128)(2,1)S(1)} collective-permute-done((bf16[2,8,384]{2,0,1:T(2,128)(2,1)S(1)}, bf16[2,8,384]{2,0,1:T(2,128)(2,1)S(1)}, u32[]{:S(2)}, u32[]{:S(2)}) %collective-permute-start.8) | collective-permute-done | bytes 12320 | tf_op jit(solution)/shard_map/ppermute | solution.py:86
  160.6 3.4 %collective-permute-start.9 = (bf16[2,8,384]{2,0,1:T(2,128)(2,1)S(1)}, bf16[2,8,384]{2,0,1:T(2,128)(2,1)S(1)}, u32[]{:S(2)}, u32[]{:S(2)}) collective-permute-start(bf16[2,8,384]{2,0,1:T(2,128)(2,1)S(1)} %copy-done.13), channel_id=1, source_target_pairs={{0,10},{1,11},{2,8},{3,9},{4,14},{5,15},{6,12},{7,13},{8,2},{9,3},... | collective-permute-start | bytes 36872 | tf_op jit(solution)/shard_map/ppermute | solution.py:86
  164.0 6.1 %collective-permute-done.9 = bf16[2,8,384]{2,0,1:T(2,128)(2,1)S(1)} collective-permute-done((bf16[2,8,384]{2,0,1:T(2,128)(2,1)S(1)}, bf16[2,8,384]{2,0,1:T(2,128)(2,1)S(1)}, u32[]{:S(2)}, u32[]{:S(2)}) %collective-permute-start.9) | collective-permute-done | bytes 12320 | tf_op jit(solution)/shard_map/ppermute | solution.py:86
  170.1 5.0 %collective-permute-start.10 = (bf16[2,8,384]{2,0,1:T(2,128)(2,1)S(1)}, bf16[2,8,384]{2,0,1:T(2,128)(2,1)S(1)}, u32[]{:S(2)}, u32[]{:S(2)}) collective-permute-start(bf16[2,8,384]{2,0,1:T(2,128)(2,1)S(1)} %copy-done.12), channel_id=1, source_target_pairs={{0,11},{1,10},{2,9},{3,8},{4,15},{5,14},{6,13},{7,12},{8,3},{9,2},... | collective-permute-start | bytes 36872 | tf_op jit(solution)/shard_map/ppermute | solution.py:86
  175.2 4.1 %collective-permute-done.10 = bf16[2,8,384]{2,0,1:T(2,128)(2,1)S(1)} collective-permute-done((bf16[2,8,384]{2,0,1:T(2,128)(2,1)S(1)}, bf16[2,8,384]{2,0,1:T(2,128)(2,1)S(1)}, u32[]{:S(2)}, u32[]{:S(2)}) %collective-permute-start.10) | collective-permute-done | bytes 12320 | tf_op jit(solution)/shard_map/ppermute | solution.py:86
  181.2 4.0 %reshape.455 = bf16[9,16,2,12,24]{3,2,1,4,0:T(2,128)(2,1)S(1)} reshape(bf16[9,384,24]{1,2,0:T(8,128)(2,1)S(1)} %reduce_sum.33) | data formatting | bytes 331776 | tf_op jit(solution)/shard_map/reshape | solution.py:120
  185.2 2.6 %copy.183 = bf16[2,16,9,12,24]{4,1,3,2,0:T(8,128)(2,1)S(1)} copy(bf16[2,16,9,12,24]{3,0,1,4,2:T(2,128)(2,1)S(1)} %bitcast.133) | data formatting | bytes 331776 | tf_op jit(solution)/shard_map/transpose | solution.py:119
  189.0 3.8 %all_to_all.30 = bf16[2,2,20736]{2,1,0:T(2,128)(2,1)S(1)} all-to-all(bf16[2,2,20736]{2,1,0:T(2,128)(2,1)S(1)} %reshape.463), channel_id=1, replica_groups=mesh['z'=16,'c'=2,'freq'=16] {'c'}, dimensions={0} | all-to-all | bytes 331776 | tf_op jit(solution)/shard_map/all_to_all | solution.py:123
  195.6 17.4 %all-to-all-start.3 = ((bf16[16,2,1296]{2,1,0:T(2,128)(2,1)}), bf16[16,2,1296]{2,1,0:T(2,128)(2,1)S(1)}, u32[]{:S(2)}, u32[]{:S(2)}) async-start(bf16[16,2,1296]{2,1,0:T(2,128)(2,1)} %reshape.465), calls=%async_computation.3 | async-start | bytes 180224 | tf_op jit(solution)/shard_map/all_to_all | solution.py:125
  214.5 12.2 %all-to-all-done.3 = bf16[16,2,1296]{2,1,0:T(2,128)(2,1)S(1)} async-done(((bf16[16,2,1296]{2,1,0:T(2,128)(2,1)}), bf16[16,2,1296]{2,1,0:T(2,128)(2,1)S(1)}, u32[]{:S(2)}, u32[]{:S(2)}) %all-to-all-start.3) | async-done | bytes 82976 | tf_op jit(solution)/shard_map/all_to_all | solution.py:125
  (107 shorter events, 22.5 us)
Async XLA Ops:
  0.6 3.0 %copy-start.23 = (bf16[2,384,1024]{2,1,0:T(8,128)(2,1)S(1)}, bf16[2,384,1024]{2,1,0:T(8,128)(2,1)}, u32[]{:S(2)}) copy-start(bf16[2,384,1024]{2,1,0:T(8,128)(2,1)} %param.6) | copy-start | bytes 4718596
  4.4 12.3 %copy-start.22 = (s32[64]{0:T(128)S(1)}, s32[64]{0:T(128)}, u32[]{:S(2)}) copy-start(s32[64]{0:T(128)} %param.8) | copy-start | bytes 772
  6.6 17.5 %copy-start = (bf16[4,2,384,384]{3,2,1,0:T(8,128)(2,1)S(1)}, bf16[4,2,384,384]{3,2,1,0:T(8,128)(2,1)}, u32[]{:S(2)}) copy-start(bf16[4,2,384,384]{3,2,1,0:T(8,128)(2,1)} %param.9) | copy-start | bytes 7077892
  7.8 14.7 %all-to-all-start = ((bf16[2,2,128,384]{3,1,0,2:T(2,128)(2,1)}), bf16[2,2,128,384]{3,1,0,2:T(2,128)(2,1)S(1)}, u32[]{:S(2)}, u32[]{:S(2)}) async-start(bf16[2,2,128,384]{3,1,0,2:T(2,128)(2,1)} %copy.152), calls=%async_computation | async-start | bytes 786432 | tf_op jit(solution)/shard_map/all_to_all | solution.py:53
  24.1 2.2 copy-start.2
  35.7 2.9 %copy-start.4 = (bf16[1,32,4,1,384]{4,0,3,2,1:T(2,128)(2,1)S(1)}, bf16[1,32,4,1,384]{4,0,3,2,1:T(2,128)(2,1)}, u32[]{:S(2)}) copy-start(bf16[1,32,4,1,384]{4,0,3,2,1:T(2,128)(2,1)} %get-tuple-element.15) | copy-start | bytes 294916
  35.7 3.4 %copy-start.3 = (bf16[1,32,4,1,384]{4,0,3,2,1:T(2,128)(2,1)S(1)}, bf16[1,32,4,1,384]{4,0,3,2,1:T(2,128)(2,1)}, u32[]{:S(2)}) copy-start(bf16[1,32,4,1,384]{4,0,3,2,1:T(2,128)(2,1)} %get-tuple-element.14) | copy-start | bytes 294916
  37.2 3.1 %copy-start.9 = (bf16[32,4,1,384]{3,0,1,2:T(8,128)(2,1)S(1)}, bf16[32,4,1,384]{3,0,1,2:T(8,128)(2,1)}, u32[]{:S(2)}) copy-start(bf16[32,4,1,384]{3,0,1,2:T(8,128)(2,1)} %fusion.86) | copy-start | bytes 294916
  37.2 3.1 %copy-start.10 = (bf16[32,4,1,384]{3,0,1,2:T(8,128)(2,1)S(1)}, bf16[32,4,1,384]{3,0,1,2:T(8,128)(2,1)}, u32[]{:S(2)}) copy-start(bf16[32,4,1,384]{3,0,1,2:T(8,128)(2,1)} %fusion.85) | copy-start | bytes 294916
  40.3 20.3 %copy-start.7 = (bf16[4,32,384]{2,1,0:T(8,128)(2,1)S(1)}, bf16[4,32,384]{2,1,0:T(8,128)(2,1)}, u32[]{:S(2)}) copy-start(bf16[4,32,384]{2,1,0:T(8,128)(2,1)} %fusion.61) | copy-start | bytes 294916
  41.2 172.5 %collective-permute-start.14 = (bf16[2,8,384]{2,0,1:T(2,128)(2,1)S(1)}, bf16[2,8,384]{2,0,1:T(2,128)(2,1)}, u32[]{:S(2)}, u32[]{:S(2)}) collective-permute-start(bf16[2,8,384]{2,0,1:T(2,128)(2,1)S(1)} %get-tuple-element.18), channel_id=1, source_target_pairs={{0,15},{1,14},{2,13},{3,12},{4,11},{5,10},{6,9},{7,8},{8,7},{9,6},... | collective-permute-start | bytes 36872 | tf_op jit(solution)/shard_map/ppermute | solution.py:86
  45.9 167.1 %collective-permute-start.13 = (bf16[2,8,384]{2,0,1:T(2,128)(2,1)}, bf16[2,8,384]{2,0,1:T(2,128)(2,1)}, u32[]{:S(2)}, u32[]{:S(2)}) collective-permute-start(bf16[2,8,384]{2,0,1:T(2,128)(2,1)} %get-tuple-element.19), channel_id=1, source_target_pairs={{0,14},{1,15},{2,12},{3,13},{4,10},{5,11},{6,8},{7,9},{8,6},{9,7},... | collective-permute-start | bytes 36872 | tf_op jit(solution)/shard_map/ppermute | solution.py:86
  49.2 130.8 %collective-permute-start.12 = (bf16[2,8,384]{2,0,1:T(2,128)(2,1)}, bf16[2,8,384]{2,0,1:T(2,128)(2,1)}, u32[]{:S(2)}, u32[]{:S(2)}) collective-permute-start(bf16[2,8,384]{2,0,1:T(2,128)(2,1)} %get-tuple-element.20), channel_id=1, source_target_pairs={{0,13},{1,12},{2,15},{3,14},{4,9},{5,8},{6,11},{7,10},{8,5},{9,4},... | collective-permute-start | bytes 36872 | tf_op jit(solution)/shard_map/ppermute | solution.py:86
  52.5 126.8 %collective-permute-start.11 = (bf16[2,8,384]{2,0,1:T(2,128)(2,1)}, bf16[2,8,384]{2,0,1:T(2,128)(2,1)}, u32[]{:S(2)}, u32[]{:S(2)}) collective-permute-start(bf16[2,8,384]{2,0,1:T(2,128)(2,1)} %get-tuple-element.21), channel_id=1, source_target_pairs={{0,12},{1,13},{2,14},{3,15},{4,8},{5,9},{6,10},{7,11},{8,4},{9,5},... | collective-permute-start | bytes 36872 | tf_op jit(solution)/shard_map/ppermute | solution.py:86
  55.4 28.4 %collective-permute-start = (bf16[2,8,384]{2,0,1:T(2,128)(2,1)}, bf16[2,8,384]{2,0,1:T(2,128)(2,1)}, u32[]{:S(2)}, u32[]{:S(2)}) collective-permute-start(bf16[2,8,384]{2,0,1:T(2,128)(2,1)} %get-tuple-element.32), channel_id=1, source_target_pairs={{0,1},{1,0},{2,3},{3,2},{4,5},{5,4},{6,7},{7,6},{8,9},{9,8},{10,11... | collective-permute-start | bytes 36872 | tf_op jit(solution)/shard_map/ppermute | solution.py:86
  58.6 4.4 %copy-start.1 = (f32[32,4,16,24]{3,2,0,1:T(8,128)S(1)}, f32[32,4,16,24]{3,2,0,1:T(8,128)}, u32[]{:S(2)}) copy-start(f32[32,4,16,24]{3,2,0,1:T(8,128)} %mul.452) | copy-start | bytes 589828
  65.2 2.0 copy-start.5
  65.2 2.0 copy-start.6
  67.3 1.1 copy-start.8
  74.6 9.2 %copy-start.21 = (bf16[2,8,384]{2,0,1:T(2,128)(2,1)S(1)}, bf16[2,8,384]{2,0,1:T(2,128)(2,1)}, u32[]{:S(2)}) copy-start(bf16[2,8,384]{2,0,1:T(2,128)(2,1)} %get-tuple-element.31) | copy-start | bytes 36868
  74.6 34.9 %copy-start.20 = (bf16[2,8,384]{2,0,1:T(2,128)(2,1)S(1)}, bf16[2,8,384]{2,0,1:T(2,128)(2,1)}, u32[]{:S(2)}) copy-start(bf16[2,8,384]{2,0,1:T(2,128)(2,1)} %get-tuple-element.30) | copy-start | bytes 36868
  74.6 41.7 %copy-start.19 = (bf16[2,8,384]{2,0,1:T(2,128)(2,1)S(1)}, bf16[2,8,384]{2,0,1:T(2,128)(2,1)}, u32[]{:S(2)}) copy-start(bf16[2,8,384]{2,0,1:T(2,128)(2,1)} %get-tuple-element.29) | copy-start | bytes 36868
  74.6 47.3 %copy-start.18 = (bf16[2,8,384]{2,0,1:T(2,128)(2,1)S(1)}, bf16[2,8,384]{2,0,1:T(2,128)(2,1)}, u32[]{:S(2)}) copy-start(bf16[2,8,384]{2,0,1:T(2,128)(2,1)} %get-tuple-element.28) | copy-start | bytes 36868
  74.6 53.8 %copy-start.17 = (bf16[2,8,384]{2,0,1:T(2,128)(2,1)S(1)}, bf16[2,8,384]{2,0,1:T(2,128)(2,1)}, u32[]{:S(2)}) copy-start(bf16[2,8,384]{2,0,1:T(2,128)(2,1)} %get-tuple-element.27) | copy-start | bytes 36868
  74.6 61.7 %copy-start.16 = (bf16[2,8,384]{2,0,1:T(2,128)(2,1)S(1)}, bf16[2,8,384]{2,0,1:T(2,128)(2,1)}, u32[]{:S(2)}) copy-start(bf16[2,8,384]{2,0,1:T(2,128)(2,1)} %get-tuple-element.26) | copy-start | bytes 36868
  74.6 69.4 %copy-start.15 = (bf16[2,8,384]{2,0,1:T(2,128)(2,1)S(1)}, bf16[2,8,384]{2,0,1:T(2,128)(2,1)}, u32[]{:S(2)}) copy-start(bf16[2,8,384]{2,0,1:T(2,128)(2,1)} %get-tuple-element.25) | copy-start | bytes 36868
  74.7 78.0 %copy-start.14 = (bf16[2,8,384]{2,0,1:T(2,128)(2,1)S(1)}, bf16[2,8,384]{2,0,1:T(2,128)(2,1)}, u32[]{:S(2)}) copy-start(bf16[2,8,384]{2,0,1:T(2,128)(2,1)} %get-tuple-element.24) | copy-start | bytes 36868
  74.7 86.0 %copy-start.13 = (bf16[2,8,384]{2,0,1:T(2,128)(2,1)S(1)}, bf16[2,8,384]{2,0,1:T(2,128)(2,1)}, u32[]{:S(2)}) copy-start(bf16[2,8,384]{2,0,1:T(2,128)(2,1)} %get-tuple-element.23) | copy-start | bytes 36868
  74.7 95.4 %copy-start.12 = (bf16[2,8,384]{2,0,1:T(2,128)(2,1)S(1)}, bf16[2,8,384]{2,0,1:T(2,128)(2,1)}, u32[]{:S(2)}) copy-start(bf16[2,8,384]{2,0,1:T(2,128)(2,1)} %get-tuple-element.22) | copy-start | bytes 36868
  74.7 106.1 %all-to-all-start.1 = ((bf16[16,9,384,24]{2,3,1,0:T(8,128)(2,1)}), bf16[16,9,384,24]{2,3,1,0:T(8,128)(2,1)S(1)}, u32[]{:S(2)}, u32[]{:S(2)}) async-start(bf16[16,9,384,24]{2,3,1,0:T(8,128)(2,1)} %copy.182), calls=%async_computation.1 | async-start | bytes 5308416 | tf_op jit(solution)/shard_map/all_to_all | solution.py:115
  83.8 25.7 %collective-permute-start.1 = (bf16[2,8,384]{2,0,1:T(2,128)(2,1)S(1)}, bf16[2,8,384]{2,0,1:T(2,128)(2,1)S(1)}, u32[]{:S(2)}, u32[]{:S(2)}) collective-permute-start(bf16[2,8,384]{2,0,1:T(2,128)(2,1)S(1)} %copy-done.21), channel_id=1, source_target_pairs={{0,2},{1,3},{2,0},{3,1},{4,6},{5,7},{6,4},{7,5},{8,10},{9,11},{10,... | collective-permute-start | bytes 36872 | tf_op jit(solution)/shard_map/ppermute | solution.py:86
  109.5 6.8 %collective-permute-start.2 = (bf16[2,8,384]{2,0,1:T(2,128)(2,1)S(1)}, bf16[2,8,384]{2,0,1:T(2,128)(2,1)S(1)}, u32[]{:S(2)}, u32[]{:S(2)}) collective-permute-start(bf16[2,8,384]{2,0,1:T(2,128)(2,1)S(1)} %copy-done.20), channel_id=1, source_target_pairs={{0,3},{1,2},{2,1},{3,0},{4,7},{5,6},{6,5},{7,4},{8,11},{9,10},{10,... | collective-permute-start | bytes 36872 | tf_op jit(solution)/shard_map/ppermute | solution.py:86
  116.3 5.6 %collective-permute-start.3 = (bf16[2,8,384]{2,0,1:T(2,128)(2,1)S(1)}, bf16[2,8,384]{2,0,1:T(2,128)(2,1)S(1)}, u32[]{:S(2)}, u32[]{:S(2)}) collective-permute-start(bf16[2,8,384]{2,0,1:T(2,128)(2,1)S(1)} %copy-done.19), channel_id=1, source_target_pairs={{0,4},{1,5},{2,6},{3,7},{4,0},{5,1},{6,2},{7,3},{8,12},{9,13},{10,... | collective-permute-start | bytes 36872 | tf_op jit(solution)/shard_map/ppermute | solution.py:86
  121.9 6.5 %collective-permute-start.4 = (bf16[2,8,384]{2,0,1:T(2,128)(2,1)S(1)}, bf16[2,8,384]{2,0,1:T(2,128)(2,1)S(1)}, u32[]{:S(2)}, u32[]{:S(2)}) collective-permute-start(bf16[2,8,384]{2,0,1:T(2,128)(2,1)S(1)} %copy-done.18), channel_id=1, source_target_pairs={{0,5},{1,4},{2,7},{3,6},{4,1},{5,0},{6,3},{7,2},{8,13},{9,12},{10,... | collective-permute-start | bytes 36872 | tf_op jit(solution)/shard_map/ppermute | solution.py:86
  128.4 8.0 %collective-permute-start.5 = (bf16[2,8,384]{2,0,1:T(2,128)(2,1)S(1)}, bf16[2,8,384]{2,0,1:T(2,128)(2,1)S(1)}, u32[]{:S(2)}, u32[]{:S(2)}) collective-permute-start(bf16[2,8,384]{2,0,1:T(2,128)(2,1)S(1)} %copy-done.17), channel_id=1, source_target_pairs={{0,6},{1,7},{2,4},{3,5},{4,2},{5,3},{6,0},{7,1},{8,14},{9,15},{10,... | collective-permute-start | bytes 36872 | tf_op jit(solution)/shard_map/ppermute | solution.py:86
  136.4 7.7 %collective-permute-start.6 = (bf16[2,8,384]{2,0,1:T(2,128)(2,1)S(1)}, bf16[2,8,384]{2,0,1:T(2,128)(2,1)S(1)}, u32[]{:S(2)}, u32[]{:S(2)}) collective-permute-start(bf16[2,8,384]{2,0,1:T(2,128)(2,1)S(1)} %copy-done.16), channel_id=1, source_target_pairs={{0,7},{1,6},{2,5},{3,4},{4,3},{5,2},{6,1},{7,0},{8,15},{9,14},{10,... | collective-permute-start | bytes 36872 | tf_op jit(solution)/shard_map/ppermute | solution.py:86
  144.1 8.6 %collective-permute-start.7 = (bf16[2,8,384]{2,0,1:T(2,128)(2,1)S(1)}, bf16[2,8,384]{2,0,1:T(2,128)(2,1)S(1)}, u32[]{:S(2)}, u32[]{:S(2)}) collective-permute-start(bf16[2,8,384]{2,0,1:T(2,128)(2,1)S(1)} %copy-done.15), channel_id=1, source_target_pairs={{0,8},{1,9},{2,10},{3,11},{4,12},{5,13},{6,14},{7,15},{8,0},{9,1},... | collective-permute-start | bytes 36872 | tf_op jit(solution)/shard_map/ppermute | solution.py:86
  152.6 8.0 %collective-permute-start.8 = (bf16[2,8,384]{2,0,1:T(2,128)(2,1)S(1)}, bf16[2,8,384]{2,0,1:T(2,128)(2,1)S(1)}, u32[]{:S(2)}, u32[]{:S(2)}) collective-permute-start(bf16[2,8,384]{2,0,1:T(2,128)(2,1)S(1)} %copy-done.14), channel_id=1, source_target_pairs={{0,9},{1,8},{2,11},{3,10},{4,13},{5,12},{6,15},{7,14},{8,1},{9,0},... | collective-permute-start | bytes 36872 | tf_op jit(solution)/shard_map/ppermute | solution.py:86
  160.6 9.5 %collective-permute-start.9 = (bf16[2,8,384]{2,0,1:T(2,128)(2,1)S(1)}, bf16[2,8,384]{2,0,1:T(2,128)(2,1)S(1)}, u32[]{:S(2)}, u32[]{:S(2)}) collective-permute-start(bf16[2,8,384]{2,0,1:T(2,128)(2,1)S(1)} %copy-done.13), channel_id=1, source_target_pairs={{0,10},{1,11},{2,8},{3,9},{4,14},{5,15},{6,12},{7,13},{8,2},{9,3},... | collective-permute-start | bytes 36872 | tf_op jit(solution)/shard_map/ppermute | solution.py:86
  170.1 9.2 %collective-permute-start.10 = (bf16[2,8,384]{2,0,1:T(2,128)(2,1)S(1)}, bf16[2,8,384]{2,0,1:T(2,128)(2,1)S(1)}, u32[]{:S(2)}, u32[]{:S(2)}) collective-permute-start(bf16[2,8,384]{2,0,1:T(2,128)(2,1)S(1)} %copy-done.12), channel_id=1, source_target_pairs={{0,11},{1,10},{2,9},{3,8},{4,15},{5,14},{6,13},{7,12},{8,3},{9,2},... | collective-permute-start | bytes 36872 | tf_op jit(solution)/shard_map/ppermute | solution.py:86
  195.6 31.1 %all-to-all-start.3 = ((bf16[16,2,1296]{2,1,0:T(2,128)(2,1)}), bf16[16,2,1296]{2,1,0:T(2,128)(2,1)S(1)}, u32[]{:S(2)}, u32[]{:S(2)}) async-start(bf16[16,2,1296]{2,1,0:T(2,128)(2,1)} %reshape.465), calls=%async_computation.3 | async-start | bytes 180224 | tf_op jit(solution)/shard_map/all_to_all | solution.py:125
  214.5 13.7 %copy-start.11 = (bf16[2,128,384]{2,1,0:T(8,128)(2,1)}, bf16[2,128,384]{2,1,0:T(8,128)(2,1)S(1)}, u32[]{:S(2)}) copy-start(bf16[2,128,384]{2,1,0:T(8,128)(2,1)S(1)} %copy_dynamic-update-slice_fusion) | copy-start | bytes 589828
